TPU v7x, 128 devices: a whole 4x4x4 slice. The times are simulated.
128 devices in a mesh: dp: 4 (over z_hi, core), mp: 32 (over x, y, z_lo).
Axes of the slice: x: 4, y: 4, z: 4 (z_hi: 2, z_lo: 2; z = z_hi * 2 + z_lo), core: 2. Of those that a mesh axis runs over, the one named last changes fastest.
Arguments:
- residual_input: bfloat16 [2048, 4608], P(('dp', 'mp')), may hold values from -6 to 6
- before_attention_gain: float32 [4608], replicated, may hold values from 0.25 to 1.75
- after_attention_gain: float32 [4608], replicated, may hold values from 0.25 to 1.75
- before_feedforward_gain: float32 [4608], replicated, may hold values from 0.25 to 1.75
- after_feedforward_gain: float32 [4608], replicated, may hold values from 0.25 to 1.75
- query_weight: bfloat16 [4608, 4096], P(None, 'mp'), may hold values from -0.09375 to 0.09375
- key_value_weight: bfloat16 [4608, 2, 32, 128], P(None, None, 'mp'), as said below
- output_weight: bfloat16 [4096, 4608], P('mp'), may hold values from -0.09375 to 0.09375
- gate_matrix: bfloat16 [4608, 20480], P(None, 'mp'), may hold values from -0.09375 to 0.09375
- up_matrix: bfloat16 [4608, 20480], P(None, 'mp'), may hold values from -0.09375 to 0.09375
- down_matrix: bfloat16 [20480, 4608], P('mp'), may hold values from -0.0390625 to 0.0390625
- key_value_cache: bfloat16 [256, 2, 32, 16, 128], P('dp', None, 'mp'), as said below
- projected_lowrank_left: bfloat16 [64, 4608, 16], P('mp'), may hold values from -0.09375 to 0.09375
- projected_lowrank_right: bfloat16 [64, 16, 3, 32, 128], P(None, None, None, 'mp'), as said below
- result_lowrank_left: bfloat16 [64, 4096, 16], P(None, 'mp'), may hold values from -0.09375 to 0.09375
- result_lowrank_right: bfloat16 [64, 16, 4608], P('mp'), may hold values from -1.5 to 1.5
- token_request: int32 [4, 512], P('dp'), may hold values from 0 to 7, never falling along the last dimension, each value on 1 to 256 neighbouring positions
- lowrank_choice_by_prompt: int32 [4, 8], P('dp'), may hold values from 0 to 63
- adapter_position: int32 [64], replicated, may hold values from 0 to 63, each once
- request_pages: int32 [4, 8, 4], replicated, may hold values from 0 to 255
Outputs:
- hidden_out: bfloat16 [2048, 4608], P(('dp', 'mp'))
- kv_new: bfloat16 [2048, 2, 32, 128], P('dp', None, 'mp')
Inputs may be any that keep to these rules, and one draw needn't show every extreme that they name: `key_value_weight`: query heads h and h2 with h // 2 == h2 // 2 have equal key and value weights: they share one key and value head. `key_value_cache`: query heads that share a key and value head have equal cached keys and values. `projected_lowrank_right`: the key and value parts of query heads that share a key and value head are equal. `token_request`: numbers never fall along a group; every request has at least one token. `adapter_position`: each slot once. `request_pages`: pages may repeat within and across requests.
All inputs are finite; a program needn't handle non-finite values.
Results may differ from a plain program's by a relative error of at most 0.035.
Values may be sent and summed in bfloat16 or wider, within the bound.
No kernel may reach another device: no remote copies, remote signals or barrier semaphores. Data moves between devices by JAX's collectives and lax.ppermute only.
A program may use at most 128 MiB of HBM per device.

v0:
```python
import math
import jax
import jax.numpy as jnp
from jax import lax
from jax.sharding import PartitionSpec as P

HIDDEN_BREADTH = 4608
ASKING_CHANNELS = 32
CHANNEL_LENGTH = 128
NUM_LOW_TERMS = 64
LOW_DIMENSION = 16
SHARD_PROMPTS = 8
PPR = 4
PAGE = 16
EPS = 1e-06
SOFTCAP = 50.0


def rms_scale(values, scaling):
    mean_square = jnp.mean(values * values, axis=-1, keepdims=True)
    return values * lax.rsqrt(mean_square + EPS) * scaling


def apply_rotary(values, token_positions):
    half_dim = values.shape[-1] // 2
    frequency = 10000.0 ** (-2.0 * jnp.arange(half_dim, dtype=jnp.float32) / values.shape[-1])
    angles = token_positions.astype(jnp.float32)[:, None] * frequency[None, :]
    cosine = jnp.cos(angles)[:, None, :]
    sine_part = jnp.sin(angles)[:, None, :]
    first_half = values[..., :half_dim]
    second_half = values[..., half_dim:]
    return jnp.concatenate(
        [
            first_half * cosine - second_half * sine_part,
            second_half * cosine + first_half * sine_part,
        ],
        axis=-1,
    )


def positions_of(segments):
    length = segments.shape[0]
    earlier = jnp.sum((segments[None, :] < segments[:, None]).astype(jnp.int32), axis=1)
    return PPR * PAGE + jnp.arange(length, dtype=jnp.int32) - earlier


def capped(scores):
    return SOFTCAP * jnp.tanh(scores / SOFTCAP)


def attend_local(query_rows, keys_new, fresh_values, keys_pre, values_pre, segments):
    scale_factor = 1.0 / math.sqrt(HIDDEN_BREADTH // ASKING_CHANNELS)
    length = segments.shape[0]
    prefix_owner = jnp.arange(keys_pre.shape[1], dtype=jnp.int32) // (PPR * PAGE)
    mask_pre = (prefix_owner[None, :] == segments[:, None])[None]
    ordinal = jnp.arange(length, dtype=jnp.int32)
    mask_new = ((segments[None, :] == segments[:, None]) & (ordinal[None, :] <= ordinal[:, None]))[
        None
    ]
    scores_pre = (
        jnp.einsum("thd,hjd->htj", query_rows, keys_pre, preferred_element_type=jnp.float32)
        * scale_factor
    )
    scores_new = (
        jnp.einsum("thd,uhd->htu", query_rows, keys_new, preferred_element_type=jnp.float32)
        * scale_factor
    )
    weight_pre = jnp.where(mask_pre, jnp.exp(capped(scores_pre)), 0.0)
    weight_new = jnp.where(mask_new, jnp.exp(capped(scores_new)), 0.0)
    totals = jnp.sum(weight_pre, axis=-1, keepdims=True) + jnp.sum(
        weight_new, axis=-1, keepdims=True
    )
    probs_pre = (weight_pre / totals).astype(jnp.bfloat16)
    probs_new = (weight_new / totals).astype(jnp.bfloat16)
    mixture = jnp.einsum("htj,hjd->thd", probs_pre, values_pre, preferred_element_type=jnp.float32)
    mixture = mixture + jnp.einsum(
        "htu,uhd->thd", probs_new, fresh_values, preferred_element_type=jnp.float32
    )
    return mixture.astype(jnp.bfloat16).reshape(length, -1)


def shards(
    residual_input,
    before_attention_gain,
    after_attention_gain,
    before_feedforward_gain,
    after_feedforward_gain,
    query_weight,
    key_value_weight,
    output_weight,
    gate_matrix,
    up_matrix,
    down_matrix,
    key_value_cache,
    projected_lowrank_left,
    projected_lowrank_right,
    result_lowrank_left,
    result_lowrank_right,
    token_request,
    lowrank_choice_by_prompt,
    adapter_position,
    request_pages,
):
    mp_index = lax.axis_index("mp")
    dp_index = lax.axis_index("dp")
    residual = residual_input.astype(jnp.float32)
    normed_rows = rms_scale(residual, before_attention_gain).astype(jnp.bfloat16)
    normalized_rows = lax.all_gather(normed_rows, "mp", axis=0, tiled=True)
    prompt_ordinal = normalized_rows.shape[0]
    channel_window = query_weight.shape[1] // CHANNEL_LENGTH
    query_rows = jnp.dot(normalized_rows, query_weight, preferred_element_type=jnp.float32).reshape(
        prompt_ordinal, channel_window, CHANNEL_LENGTH
    )
    key_value_rows = jnp.dot(
        normalized_rows,
        key_value_weight.reshape(HIDDEN_BREADTH, 2 * channel_window * CHANNEL_LENGTH),
        preferred_element_type=jnp.float32,
    ).reshape(prompt_ordinal, 2, channel_window, CHANNEL_LENGTH)
    segments = token_request[0]
    request_ids = lowrank_choice_by_prompt[0]
    request_range = jnp.arange(SHARD_PROMPTS, dtype=jnp.int32)
    membership = segments[:, None] == request_range[None, :]
    adapter_range = jnp.arange(NUM_LOW_TERMS, dtype=jnp.int32)
    token_adapter = jnp.sum(jnp.where(membership, request_ids[None, :], 0), axis=1)
    token_adapter_slot = jnp.sum(
        jnp.where(token_adapter[:, None] == adapter_range[None, :], adapter_position[None, :], 0),
        axis=1,
    )
    gathered_down = lax.all_gather(projected_lowrank_left, "mp", axis=0, tiled=True)
    request_slot = jnp.sum(
        jnp.where(request_ids[:, None] == adapter_range[None, :], adapter_position[None, :], 0),
        axis=1,
    )
    request_down = gathered_down[request_slot]
    request_factors = jnp.einsum(
        "td,rdk->trk", normalized_rows, request_down, preferred_element_type=jnp.float32
    )
    lowrank_source = jnp.sum(jnp.where(membership[:, :, None], request_factors, 0.0), axis=1)
    lowrank_source = lowrank_source.astype(jnp.bfloat16)
    choice_mask_table = membership.astype(jnp.bfloat16)
    broadened_lines = (choice_mask_table[:, :, None] * lowrank_source[:, None, :]).reshape(
        prompt_ordinal, SHARD_PROMPTS * LOW_DIMENSION
    )
    raised_result_lines = projected_lowrank_right[request_ids].reshape(
        SHARD_PROMPTS * LOW_DIMENSION, 3 * channel_window * CHANNEL_LENGTH
    )
    adapter_query_key_value = jnp.dot(
        broadened_lines, raised_result_lines, preferred_element_type=jnp.float32
    ).reshape(prompt_ordinal, 3, channel_window, CHANNEL_LENGTH)
    token_positions = positions_of(segments)
    rotary_queries = apply_rotary(
        query_rows + adapter_query_key_value[:, 0], token_positions
    ).astype(jnp.bfloat16)
    rotary_keys = apply_rotary(
        key_value_rows[:, 0] + adapter_query_key_value[:, 1], token_positions
    ).astype(jnp.bfloat16)
    fresh_values = (key_value_rows[:, 1] + adapter_query_key_value[:, 2]).astype(jnp.bfloat16)
    kv_new = jnp.stack([rotary_keys, fresh_values], axis=1)
    own_pages = lax.dynamic_index_in_dim(request_pages, dp_index, 0, keepdims=False).reshape(
        SHARD_PROMPTS * PPR
    )
    whole_pool = lax.all_gather(key_value_cache, "dp", axis=0, tiled=True)
    chosen = whole_pool[own_pages]
    keys_pre = jnp.transpose(chosen[:, 0], (1, 0, 2, 3)).reshape(
        channel_window, SHARD_PROMPTS * PPR * PAGE, CHANNEL_LENGTH
    )
    values_pre = jnp.transpose(chosen[:, 1], (1, 0, 2, 3)).reshape(
        channel_window, SHARD_PROMPTS * PPR * PAGE, CHANNEL_LENGTH
    )
    attended = attend_local(
        rotary_queries, rotary_keys, fresh_values, keys_pre, values_pre, segments
    )
    request_output_down = result_lowrank_left[request_ids]
    request_output_factors = jnp.einsum(
        "tc,rck->trk", attended, request_output_down, preferred_element_type=jnp.float32
    )
    output_adapter_piece = jnp.sum(
        jnp.where(membership[:, :, None], request_output_factors, 0.0), axis=1
    )
    result_lowrank_source = lax.psum(output_adapter_piece.astype(jnp.bfloat16), "mp")
    result_seat_lines = result_lowrank_right.shape[0]
    output_slots = mp_index * result_seat_lines + jnp.arange(result_seat_lines, dtype=jnp.int32)
    resident_here = (token_adapter_slot[:, None] == output_slots[None, :]).astype(jnp.bfloat16)
    broadened_result = (resident_here[:, :, None] * result_lowrank_source[:, None, :]).reshape(
        prompt_ordinal, result_seat_lines * LOW_DIMENSION
    )
    raised_window = result_lowrank_right.reshape(result_seat_lines * LOW_DIMENSION, HIDDEN_BREADTH)
    attn_sum = lax.psum_scatter(
        (
            jnp.dot(attended, output_weight, preferred_element_type=jnp.float32)
            + jnp.dot(broadened_result, raised_window, preferred_element_type=jnp.float32)
        ).astype(jnp.bfloat16),
        "mp",
        scatter_dimension=0,
        tiled=True,
    ).astype(jnp.float32)
    after_attn = (residual + rms_scale(attn_sum, after_attention_gain)).astype(jnp.bfloat16)
    normed_ffw = rms_scale(after_attn.astype(jnp.float32), before_feedforward_gain).astype(
        jnp.bfloat16
    )
    piece = lax.all_gather(normed_ffw, "mp", axis=0, tiled=True)
    gated = jnp.dot(piece, gate_matrix, preferred_element_type=jnp.float32)
    upward = jnp.dot(piece, up_matrix, preferred_element_type=jnp.float32)
    hidden = (jax.nn.gelu(gated, approximate=True) * upward).astype(jnp.bfloat16)
    ffw_sum = lax.psum_scatter(
        jnp.dot(hidden, down_matrix, preferred_element_type=jnp.float32).astype(jnp.bfloat16),
        "mp",
        scatter_dimension=0,
        tiled=True,
    ).astype(jnp.float32)
    hidden_out = (
        after_attn.astype(jnp.float32) + rms_scale(ffw_sum, after_feedforward_gain)
    ).astype(jnp.bfloat16)
    return (hidden_out, kv_new)


def solution(mesh):
    return jax.shard_map(
        shards,
        mesh=mesh,
        in_specs=(
            P(("dp", "mp"), None),
            P(),
            P(),
            P(),
            P(),
            P(None, "mp"),
            P(None, None, "mp", None),
            P("mp", None),
            P(None, "mp"),
            P(None, "mp"),
            P("mp", None),
            P("dp", None, "mp", None, None),
            P("mp", None, None),
            P(None, None, None, "mp", None),
            P(None, "mp", None),
            P("mp", None, None),
            P("dp", None),
            P("dp", None),
            P(),
            P(),
        ),
        out_specs=(P(("dp", "mp"), None), P("dp", None, "mp", None)),
        check_vma=False,
    )
```

profile of v0, /device:TPU:0, one launch (start us, length us, event | category | flops | bytes accessed | tf_op | source)
XLA Modules:
  0.0 1112.8 jit_solution(17951339612052338414)
XLA Ops:
  7.2 0.0 copy-start
  7.2 0.0 all-gather.5.cloned.1.call-start
  7.2 0.7 all-gather.5.cloned.1.call-update
  7.9 0.0 all-gather.7.cloned.1.call-start
  8.0 1.1 fusion.31
  9.0 1.7 fusion.33
  10.7 0.0 all-gather.7.cloned.1.call-update
  10.7 0.0 all-gather.9.cloned.1.call-start
  10.8 0.7 all-gather.9.cloned.1.call-update
  11.5 0.0 reduce-scatter.3.cloned.1.call-start
  11.5 0.7 constant_dynamic-slice_fusion
  12.2 0.1 copy.46
  12.3 0.1 reshape.488
  12.4 0.7 fusion.73
  13.1 2.1 gather_fusion.3
  15.2 1.7 gather_fusion.2
  16.9 0.1 copy.47
  16.9 0.8 copy.48
  17.7 2.0 copy.60
  19.7 2.5 copy.50
  22.3 0.2 select_reduce_fusion.4
  22.5 0.1 select_reduce_fusion.3
  22.6 0.1 select_reduce_fusion.2
  22.7 0.2 convert_reduce_fusion
  22.9 0.1 compare_convert_fusion
  23.0 15.9 %all-gather.5.cloned.1.call-done = bf16[256,2,1,16,128]{4,3,2,1,0:T(8,128)(2,1)} async-done(((bf16[64,2,1,16,128]{4,3,2,1,0:T(8,128)(2,1)}), bf16[256,2,1,16,128]{4,3,2,1,0:T(8,128)(2,1)}) %all-gather.5.cloned.1.call-update) | async-done | bytes 2097168 | tf_op jit(solution)/shard_map/all_gather | solution.py:162
  38.9 2.2 gather_fusion
  41.2 157.9 %all-gather.7.cloned.1.call-done = bf16[512,4608]{1,0:T(8,128)(2,1)} async-done(((bf16[16,4608]{1,0:T(8,128)(2,1)}), bf16[512,4608]{1,0:T(8,128)(2,1)}) %all-gather.7.cloned.1.call-update) | async-done | bytes 4718608 | tf_op jit(solution)/shard_map/all_gather | solution.py:108
  199.1 4.5 fusion.19
  203.6 207.7 %all-gather.9.cloned.1.call-done = bf16[64,4608,16]{1,2,0:T(8,128)(2,1)} async-done(((bf16[2,4608,16]{1,2,0:T(8,128)(2,1)}), bf16[64,4608,16]{1,2,0:T(8,128)(2,1)}) %all-gather.9.cloned.1.call-update) | async-done | bytes 9437200 | tf_op jit(solution)/shard_map/all_gather | solution.py:129
  411.2 4.3 gather_fusion.1
  415.5 0.0 copy-start.5
  415.6 0.0 copy-start.4
  415.6 4.1 fusion.84
  419.8 0.2 convolution_bitcast_fusion
  420.0 0.1 fusion.39
  420.1 1.7 fusion.22
  421.8 0.6 fusion.54
  422.4 0.5 fusion.82
  422.9 0.5 fusion.83
  423.4 0.0 copy-start.6
  423.4 0.3 fusion.26
  423.7 0.2 fusion.24
  423.9 0.2 fusion.86
  424.2 157.2 %psum.7 = bf16[512,16]{0,1:T(8,128)(2,1)S(1)} all-reduce(bf16[512,16]{0,1:T(8,128)(2,1)S(1)} %select_reduce_fusion), channel_id=1, replica_groups=mesh['dp'=4,'mp'=32] {'mp'}, use_global_device_ids=true, to_apply=%region_9.10 | all-reduce | flops 8192 | bytes 32768 | tf_op jit(solution)/shard_map/psum | solution.py:180
  581.4 1.4 fusion.63
  582.8 3.5 fusion
  586.4 0.0 reduce-scatter.3.cloned.1.call-update
  586.4 0.0 all-gather.11.cloned.1.call-start
  586.4 165.2 %reduce-scatter.3.cloned.1.call-done = bf16[16,4608]{1,0:T(8,128)(2,1)} async-done(((bf16[512,4608]{1,0:T(8,128)(2,1)}), bf16[16,4608]{1,0:T(8,128)(2,1)}) %reduce-scatter.3.cloned.1.call-update) | async-done | bytes 147472 | tf_op jit(solution)/shard_map/reduce_scatter | solution.py:188
  751.6 1.1 fusion.27
  752.7 1.2 fusion.35
  753.9 0.8 fusion.37
  754.6 0.0 all-gather.11.cloned.1.call-update
  754.7 0.2 reduce-scatter.5.cloned.1.call-start
  754.9 154.9 %all-gather.11.cloned.1.call-done = bf16[512,4608]{1,0:T(8,128)(2,1)} async-done(((bf16[16,4608]{1,0:T(8,128)(2,1)}), bf16[512,4608]{1,0:T(8,128)(2,1)}) %all-gather.11.cloned.1.call-update) | async-done | bytes 4718608 | tf_op jit(solution)/shard_map/all_gather | solution.py:201
  909.8 7.4 fusion.85
  917.2 0.0 copy-start.1
  917.2 14.2 %convolution_convert_fusion = bf16[512,4608]{1,0:T(8,128)(2,1)} fusion(bf16[640,4608]{1,0:T(8,128)(2,1)} %param.30, bf16[512,4608]{1,0:T(8,128)(2,1)} %all-gather.11.cloned.1.call-done, bf16[4608,640]{1,0:T(8,128)(2,1)} %param.29, f32[512,640]{1,0:T(8,128)S(1)} %fusion.85), kind=kOutput, calls=%fused_computation.6 | convolution fusion | flops 6045433856 | bytes 22544384 | tf_op jit(solution)/shard_map/dot_general | solution.py:206
  931.5 0.0 reduce-scatter.5.cloned.1.call-update
  931.5 0.9 copy.52
  932.4 170.8 %reduce-scatter.5.cloned.1.call-done = bf16[16,4608]{1,0:T(8,128)(2,1)} async-done(((bf16[512,4608]{1,0:T(8,128)(2,1)}), bf16[16,4608]{1,0:T(8,128)(2,1)}) %reduce-scatter.5.cloned.1.call-update) | async-done | bytes 147472 | tf_op jit(solution)/shard_map/reduce_scatter | solution.py:205
  1103.2 1.1 fusion.29
  1104.3 1.7 fusion.38
  (47 shorter events, 0.3 us)
Async XLA Ops:
  7.2 575.7 %copy-start = (bf16[128,4608]{1,0:T(8,128)(2,1)S(1)}, bf16[128,4608]{1,0:T(8,128)(2,1)}, u32[]{:S(2)}) copy-start(bf16[128,4608]{1,0:T(8,128)(2,1)} %param.27) | copy-start | bytes 3538948
  7.2 31.8 %all-gather.5.cloned.1.call-start = ((), (), s32[]{:S(2)}) async-start(), calls=%async_computation.2 | async-start | bytes 2621440 | tf_op jit(solution)/shard_map/all_gather | solution.py:162
  7.9 191.1 %all-gather.7.cloned.1.call-start = ((), (), s32[]{:S(2)}) async-start(), calls=%async_computation.3 | async-start | bytes 4866048 | tf_op jit(solution)/shard_map/all_gather | solution.py:108
  10.7 400.5 %all-gather.9.cloned.1.call-start = ((), (), s32[]{:S(2)}) async-start(), calls=%async_computation.4 | async-start | bytes 9732096 | tf_op jit(solution)/shard_map/all_gather | solution.py:129
  11.5 740.1 %reduce-scatter.3.cloned.1.call-start = ((), (), s32[]{:S(2)}) async-start(), calls=%async_computation.5 | async-start | bytes 4866048 | tf_op jit(solution)/shard_map/reduce_scatter | solution.py:188
  17.7 4.6 copy-start.11
  17.7 4.6 copy-start.12
  17.7 4.8 copy-start.7
  415.5 4.2 copy-start.5
  415.5 4.6 slice-start
  415.6 4.6 copy-start.4
  415.6 4.6 slice-start.1
  422.9 1.0 copy-start.2
  423.4 158.0 %copy-start.6 = (bf16[2,16,4608]{2,1,0:T(8,128)(2,1)S(1)}, bf16[2,16,4608]{2,1,0:T(8,128)(2,1)}, u32[]{:S(2)}) copy-start(bf16[2,16,4608]{2,1,0:T(8,128)(2,1)} %param.35) | copy-start | bytes 884740
  586.4 166.3 %copy-start.3 = (bf16[16,4608]{1,0:T(8,128)(2,1)S(1)}, bf16[16,4608]{1,0:T(8,128)(2,1)}, u32[]{:S(2)}) copy-start(bf16[16,4608]{1,0:T(8,128)(2,1)} %param.20) | copy-start | bytes 442372
  586.4 166.3 %copy-start.8 = (f32[4608]{0:T(1024)S(1)}, f32[4608]{0:T(1024)}, u32[]{:S(2)}) copy-start(f32[4608]{0:T(1024)} %param.22) | copy-start | bytes 55300
  586.4 167.5 %copy-start.9 = (f32[4608]{0:T(1024)S(1)}, f32[4608]{0:T(1024)}, u32[]{:S(2)}) copy-start(f32[4608]{0:T(1024)} %param.23) | copy-start | bytes 55300
  586.4 323.4 %all-gather.11.cloned.1.call-start = ((), (), s32[]{:S(2)}) async-start(), calls=%async_computation.6 | async-start | bytes 4866048 | tf_op jit(solution)/shard_map/all_gather | solution.py:201
  754.7 348.5 %reduce-scatter.5.cloned.1.call-start = ((), (), s32[]{:S(2)}) async-start(), calls=%async_computation.7 | async-start | bytes 4866048 | tf_op jit(solution)/shard_map/reduce_scatter | solution.py:205
  917.2 188.7 %copy-start.1 = (bf16[128,4608]{1,0:T(8,128)(2,1)S(1)}, bf16[128,4608]{1,0:T(8,128)(2,1)}, u32[]{:S(2)}) copy-start(bf16[128,4608]{1,0:T(8,128)(2,1)} %param.27) | copy-start | bytes 3538948
  931.5 172.8 %copy-start.10 = (f32[4608]{0:T(1024)S(1)}, f32[4608]{0:T(1024)}, u32[]{:S(2)}) copy-start(f32[4608]{0:T(1024)} %param.24) | copy-start | bytes 55300
Sparse Core Ops, SparseCore 0:
  9.7 29.2 all-gather.4
  41.1 157.8 all-gather.6
  200.7 210.4 all-gather.8
  586.5 165.0 reduce-scatter.2
  754.8 154.9 all-gather.10
  931.6 171.5 reduce-scatter.4
where the time goes:
time: 1110 us
  waiting for transfers between devices  874 us (79%)
  blocking collectives  157 us (14%)
  matrix products  38.8 us (3%)
  local copies, waits for them, and re-layouts  17.5 us (2%)
  between operations  14.5 us (1%)
    all_gather x1, waiting for transfers between devices, shards(): lax.all_gather(projected_lowrank_left, 'mp', axis=0, tiled=True)  208 us
    reduce_scatter x1, waiting for transfers between devices, shards(): lax.psum_scatter(jnp.dot(hidden, down_matrix, preferred_element_type=jnp....  171 us
    reduce_scatter x1, waiting for transfers between devices, shards(): lax.psum_scatter((jnp.dot(attended, output_weight, preferred_element_type...  165 us
    all_gather x1, waiting for transfers between devices, shards(): normalized_rows = lax.all_gather(normed_rows, 'mp', axis=0, tiled=True)  158 us
    psum x1, blocking collectives, shards(): lax.psum(output_adapter_piece.astype(jnp.bfloat16), 'mp')  157 us
    all_gather x1, waiting for transfers between devices, shards(): piece = lax.all_gather(normed_ffw, 'mp', axis=0, tiled=True)  155 us
  transfers between devices with their start and end apart: 6, of which 6 were waited for; matrix products, arithmetic and copies ran while one was open for 2% of the time, Pallas kernels for 0%

commit v1 on v0

--- a/solution.py
+++ b/solution.py
@@ -105,7 +105,14 @@
     dp_index = lax.axis_index("dp")
     residual = residual_input.astype(jnp.float32)
     normed_rows = rms_scale(residual, before_attention_gain).astype(jnp.bfloat16)
-    normalized_rows = lax.all_gather(normed_rows, "mp", axis=0, tiled=True)
+
+    def switch_chunk(mine, named_axis, dim_at):
+        clean = jnp.stack([mine for _ in range(lax.axis_size(named_axis))], 0)
+        r1 = lax.all_to_all(clean, axis_name=named_axis, split_axis=0, concat_axis=0)
+        part_now = jnp.concatenate(r1, dim_at)
+        return part_now
+
+    normalized_rows = switch_chunk(normed_rows, "mp", 0)
     prompt_ordinal = normalized_rows.shape[0]
     channel_window = query_weight.shape[1] // CHANNEL_LENGTH
     query_rows = jnp.dot(normalized_rows, query_weight, preferred_element_type=jnp.float32).reshape(

time: 1110 us -> 1000 us (0.901)
  waiting for transfers between devices: 874 us -> 754 us
    all_gather x1 -> x0, waiting for transfers between devices: 158 us -> none  [shards(): normalized_rows = lax.all_gather(normed_rows, 'mp', axis=0, tiled=True)]
    all_gather x1, waiting for transfers between devices: 15.9 us -> 54.7 us  [shards(): whole_pool = lax.all_gather(key_value_cache, 'dp', axis=0, tiled=True)]
where the time goes in v1:
time: 1000 us
  waiting for transfers between devices  754 us (75%)
  blocking collectives  157 us (16%)
  matrix products  41.2 us (4%)
  local copies, waits for them, and re-layouts  19.2 us (2%)
  between operations  14.1 us (1%)
    all_gather x1, waiting for transfers between devices, shards(): lax.all_gather(projected_lowrank_left, 'mp', axis=0, tiled=True)  200 us
    reduce_scatter x1, waiting for transfers between devices, shards(): lax.psum_scatter(jnp.dot(hidden, down_matrix, preferred_element_type=jnp....  171 us
    reduce_scatter x1, waiting for transfers between devices, shards(): lax.psum_scatter((jnp.dot(attended, output_weight, preferred_element_type...  166 us
    psum x1, blocking collectives, shards(): lax.psum(output_adapter_piece.astype(jnp.bfloat16), 'mp')  157 us
    all_gather x1, waiting for transfers between devices, shards(): piece = lax.all_gather(normed_ffw, 'mp', axis=0, tiled=True)  155 us
    all_gather x1, waiting for transfers between devices, shards(): whole_pool = lax.all_gather(key_value_cache, 'dp', axis=0, tiled=True)  54.7 us
  transfers between devices with their start and end apart: 6, of which 6 were waited for; matrix products, arithmetic and copies ran while one was open for 2% of the time, Pallas kernels for 0%

profile of v1, /device:TPU:0, one launch (start us, length us, event | category | flops | bytes accessed | tf_op | source)
XLA Modules:
  0.0 1004.3 jit_solution(13509973199017390004)
XLA Ops:
  7.2 0.0 copy-start
  7.2 0.0 all-gather.4.cloned.1.call-start
  7.2 0.7 all-gather.4.cloned.1.call-update
  7.9 0.0 all-gather.6.cloned.1.call-start
  8.0 0.7 all-gather.6.cloned.1.call-update
  8.7 1.1 fusion.26
  9.7 1.0 fusion.28
  10.8 2.7 stack.4
  13.4 9.0 all-to-all-start
  22.5 0.0 reduce-scatter.3.cloned.1.call-start
  22.5 0.7 constant_dynamic-slice_fusion
  23.2 0.1 copy.46
  23.3 0.1 reshape.493
  23.4 1.2 gather_fusion.3
  24.6 1.7 gather_fusion.2
  26.3 0.1 copy.47
  26.4 0.8 copy.48
  27.1 2.0 copy.60
  29.1 2.5 copy.50
  31.7 0.2 select_reduce_fusion.4
  31.9 0.1 select_reduce_fusion.3
  32.0 0.1 select_reduce_fusion.2
  32.1 0.2 convert_reduce_fusion
  32.3 0.1 compare_convert_fusion
  32.4 54.7 %all-gather.4.cloned.1.call-done = bf16[256,2,1,16,128]{4,3,2,1,0:T(8,128)(2,1)} async-done(((bf16[64,2,1,16,128]{4,3,2,1,0:T(8,128)(2,1)}), bf16[256,2,1,16,128]{4,3,2,1,0:T(8,128)(2,1)}) %all-gather.4.cloned.1.call-update) | async-done | bytes 2097168 | tf_op jit(solution)/shard_map/all_gather | solution.py:169
  87.1 2.2 gather_fusion
  89.3 7.0 all-to-all-done
  96.2 4.6 convolution_bitcast_fusion.1
  100.9 199.7 %all-gather.6.cloned.1.call-done = bf16[64,4608,16]{1,2,0:T(8,128)(2,1)} async-done(((bf16[2,4608,16]{1,2,0:T(8,128)(2,1)}), bf16[64,4608,16]{1,2,0:T(8,128)(2,1)}) %all-gather.6.cloned.1.call-update) | async-done | bytes 9437200 | tf_op jit(solution)/shard_map/all_gather | solution.py:136
  300.6 4.3 gather_fusion.1
  304.9 0.0 copy-start.5
  304.9 0.0 copy-start.4
  304.9 4.1 fusion.79
  309.0 0.2 convolution_bitcast_fusion
  309.3 4.0 fusion.17
  313.3 0.1 fusion.34
  313.4 0.6 fusion.49
  314.0 0.5 fusion.77
  314.5 0.0 copy-start.2
  314.5 0.5 fusion.78
  315.0 0.0 copy-start.6
  315.0 0.3 fusion.21
  315.2 0.2 fusion.19
  315.5 0.2 fusion.81
  315.7 157.2 %psum.7 = bf16[512,16]{0,1:T(8,128)(2,1)S(1)} all-reduce(bf16[512,16]{0,1:T(8,128)(2,1)S(1)} %select_reduce_fusion), channel_id=1, replica_groups=mesh['dp'=4,'mp'=32] {'mp'}, use_global_device_ids=true, to_apply=%region_9.10 | all-reduce | flops 8192 | bytes 32768 | tf_op jit(solution)/shard_map/psum | solution.py:187
  473.0 1.4 fusion.58
  474.4 3.5 fusion
  477.9 0.0 reduce-scatter.3.cloned.1.call-update
  478.0 0.0 all-gather.8.cloned.1.call-start
  478.0 165.5 %reduce-scatter.3.cloned.1.call-done = bf16[16,4608]{1,0:T(8,128)(2,1)} async-done(((bf16[512,4608]{1,0:T(8,128)(2,1)}), bf16[16,4608]{1,0:T(8,128)(2,1)}) %reduce-scatter.3.cloned.1.call-update) | async-done | bytes 147472 | tf_op jit(solution)/shard_map/reduce_scatter | solution.py:195
  643.5 1.1 fusion.22
  644.6 1.2 fusion.30
  645.8 0.8 fusion.32
  646.5 0.0 all-gather.8.cloned.1.call-update
  646.6 0.2 reduce-scatter.5.cloned.1.call-start
  646.8 154.7 %all-gather.8.cloned.1.call-done = bf16[512,4608]{1,0:T(8,128)(2,1)} async-done(((bf16[16,4608]{1,0:T(8,128)(2,1)}), bf16[512,4608]{1,0:T(8,128)(2,1)}) %all-gather.8.cloned.1.call-update) | async-done | bytes 4718608 | tf_op jit(solution)/shard_map/all_gather | solution.py:208
  801.5 7.4 fusion.80
  808.9 0.0 copy-start.1
  808.9 14.2 %convolution_convert_fusion = bf16[512,4608]{1,0:T(8,128)(2,1)} fusion(bf16[640,4608]{1,0:T(8,128)(2,1)} %param.30, bf16[512,4608]{1,0:T(8,128)(2,1)} %all-gather.8.cloned.1.call-done, bf16[4608,640]{1,0:T(8,128)(2,1)} %param.29, f32[512,640]{1,0:T(8,128)S(1)} %fusion.80), kind=kOutput, calls=%fused_computation.6 | convolution fusion | flops 6045433856 | bytes 22544384 | tf_op jit(solution)/shard_map/dot_general | solution.py:213
  823.2 0.0 reduce-scatter.5.cloned.1.call-update
  823.2 0.9 copy.52
  824.1 170.9 %reduce-scatter.5.cloned.1.call-done = bf16[16,4608]{1,0:T(8,128)(2,1)} async-done(((bf16[512,4608]{1,0:T(8,128)(2,1)}), bf16[16,4608]{1,0:T(8,128)(2,1)}) %reduce-scatter.5.cloned.1.call-update) | async-done | bytes 147472 | tf_op jit(solution)/shard_map/reduce_scatter | solution.py:212
  995.0 1.1 fusion.24
  996.1 1.7 fusion.33
  (44 shorter events, 0.3 us)
Async XLA Ops:
  7.2 467.2 %copy-start = (bf16[128,4608]{1,0:T(8,128)(2,1)S(1)}, bf16[128,4608]{1,0:T(8,128)(2,1)}, u32[]{:S(2)}) copy-start(bf16[128,4608]{1,0:T(8,128)(2,1)} %param.27) | copy-start | bytes 3538948
  7.2 79.9 %all-gather.4.cloned.1.call-start = ((), (), s32[]{:S(2)}) async-start(), calls=%async_computation.3 | async-start | bytes 2621440 | tf_op jit(solution)/shard_map/all_gather | solution.py:169
  7.9 292.6 %all-gather.6.cloned.1.call-start = ((), (), s32[]{:S(2)}) async-start(), calls=%async_computation.4 | async-start | bytes 9732096 | tf_op jit(solution)/shard_map/all_gather | solution.py:136
  13.4 10.0 copy-start.12
  13.4 10.0 copy-start.7
  13.4 82.8 %all-to-all-start = ((bf16[32,16,4608]{2,1,0:T(8,128)(2,1)}), bf16[32,16,4608]{2,1,0:T(8,128)(2,1)}, u32[]{:S(2)}, u32[]{:S(2)}) async-start(bf16[32,16,4608]{2,1,0:T(8,128)(2,1)} %stack.4), calls=%async_computation | async-start | bytes 9437184 | tf_op jit(solution)/shard_map/all_to_all | solution.py:111
  22.5 621.0 %reduce-scatter.3.cloned.1.call-start = ((), (), s32[]{:S(2)}) async-start(), calls=%async_computation.5 | async-start | bytes 4866048 | tf_op jit(solution)/shard_map/reduce_scatter | solution.py:195
  27.1 4.6 copy-start.13
  27.1 4.8 copy-start.8
  304.9 4.2 copy-start.5
  304.9 4.4 copy-start.4
  314.5 1.0 copy-start.2
  315.0 158.0 %copy-start.6 = (bf16[2,16,4608]{2,1,0:T(8,128)(2,1)S(1)}, bf16[2,16,4608]{2,1,0:T(8,128)(2,1)}, u32[]{:S(2)}) copy-start(bf16[2,16,4608]{2,1,0:T(8,128)(2,1)} %param.35) | copy-start | bytes 884740
  477.9 166.7 %copy-start.3 = (bf16[16,4608]{1,0:T(8,128)(2,1)S(1)}, bf16[16,4608]{1,0:T(8,128)(2,1)}, u32[]{:S(2)}) copy-start(bf16[16,4608]{1,0:T(8,128)(2,1)} %param.20) | copy-start | bytes 442372
  477.9 166.7 %copy-start.9 = (f32[4608]{0:T(1024)S(1)}, f32[4608]{0:T(1024)}, u32[]{:S(2)}) copy-start(f32[4608]{0:T(1024)} %param.22) | copy-start | bytes 55300
  477.9 167.8 %copy-start.10 = (f32[4608]{0:T(1024)S(1)}, f32[4608]{0:T(1024)}, u32[]{:S(2)}) copy-start(f32[4608]{0:T(1024)} %param.23) | copy-start | bytes 55300
  478.0 323.5 %all-gather.8.cloned.1.call-start = ((), (), s32[]{:S(2)}) async-start(), calls=%async_computation.6 | async-start | bytes 4866048 | tf_op jit(solution)/shard_map/all_gather | solution.py:208
  646.6 348.4 %reduce-scatter.5.cloned.1.call-start = ((), (), s32[]{:S(2)}) async-start(), calls=%async_computation.7 | async-start | bytes 4866048 | tf_op jit(solution)/shard_map/reduce_scatter | solution.py:212
  808.9 188.9 %copy-start.1 = (bf16[128,4608]{1,0:T(8,128)(2,1)S(1)}, bf16[128,4608]{1,0:T(8,128)(2,1)}, u32[]{:S(2)}) copy-start(bf16[128,4608]{1,0:T(8,128)(2,1)} %param.27) | copy-start | bytes 3538948
  823.2 172.9 %copy-start.11 = (f32[4608]{0:T(1024)S(1)}, f32[4608]{0:T(1024)}, u32[]{:S(2)}) copy-start(f32[4608]{0:T(1024)} %param.24) | copy-start | bytes 55300
Sparse Core Ops, SparseCore 0:
  9.7 77.3 all-gather.3
  88.7 211.8 all-gather.5
  478.1 165.3 reduce-scatter.2
  646.7 154.7 all-gather.7
  823.3 171.6 reduce-scatter.4
